TPU v7x, 512 devices: a whole 4x4x16 slice. The times are simulated.
512 devices in a mesh: gx: 8 (over z_lo, core), gy: 16 (over x, z_hi), gz: 4 (over y).
Axes of the slice: x: 4, y: 4, z: 16 (z_hi: 4, z_lo: 4; z = z_hi * 4 + z_lo), core: 2. Of those that a mesh axis runs over, the one named last changes fastest.
Arguments:
- heat_source: float32 [128, 256, 512], P('gx', 'gy', 'gz'), may hold values from -6 to 6
- material: int32 [128, 256, 512], P('gx', 'gy', 'gz'), may hold values from 0 to 2
- conductivity: float32 [3], replicated, may hold values from 0.3 to 3
Outputs:
- temperature: float32 [128, 256, 512], P('gx', 'gy', 'gz')
All inputs are finite; a program needn't handle non-finite values.
Results may differ from a plain program's by a relative error of at most 0.00002.
Values sent between devices are 32-bit elements; how exact they have to be, the bound alone decides.
No kernel may reach another device: no remote copies, remote signals or barrier semaphores. Data moves between devices by JAX's collectives and lax.ppermute only.
A program may use at most 192 MiB of HBM per device.

v0:
```python
import jax
import jax.numpy as jnp
from jax import lax
from jax.sharding import PartitionSpec as P

DEGREE = 3
LEVELS = 3
MATERIALS = 3

LOW = 0.3
HIGH = 2.0

AXES = ("gx", "gy", "gz")
HALO0 = 6
HALO1 = 8
HALO2 = 8


def exchange(blocks, widths):
    blocks = list(blocks)
    for k, axis in enumerate(AXES):
        count = lax.axis_size(axis)
        dims = [b.ndim - 3 + k for b in blocks]
        sizes = [b.shape[d] for b, d in zip(blocks, dims)]
        reach = [-(-w // n) for w, n in zip(widths, sizes)]
        lows = [[] for _ in blocks]
        highs = [[] for _ in blocks]
        for shift in range(1, max(reach) + 1):
            users = [j for j in range(len(blocks)) if reach[j] >= shift]
            takes = {j: min(sizes[j], widths[j] - (shift - 1) * sizes[j]) for j in users}
            for side in (0, 1):
                slabs = []
                for j in users:
                    n, t = sizes[j], takes[j]
                    start = n - t if side == 0 else 0
                    slabs.append(lax.slice_in_dim(blocks[j], start, start + t, axis=dims[j]))
                if shift >= count:
                    got = [jnp.zeros_like(s) for s in slabs]
                else:
                    if side == 0:
                        pairs = [(i, i + shift) for i in range(count - shift)]
                    else:
                        pairs = [(i + shift, i) for i in range(count - shift)]
                    flat = jnp.concatenate([s.reshape(-1) for s in slabs])
                    flat = lax.ppermute(flat, axis, pairs)
                    got, at = [], 0
                    for s in slabs:
                        got.append(flat[at:at + s.size].reshape(s.shape))
                        at += s.size
                for j, g in zip(users, got):
                    (lows if side == 0 else highs)[j].append(g)
        blocks = [
            jnp.concatenate(lows[j][::-1] + [blocks[j]] + highs[j], axis=dims[j])
            for j in range(len(blocks))
        ]
    return blocks


def inside_mask(block_shape, width):
    parts = []
    for k, axis in enumerate(AXES):
        n = block_shape[k]
        total = n * lax.axis_size(axis)
        coord = lax.axis_index(axis) * n - width + jnp.arange(n + 2 * width)
        parts.append((coord >= 0) & (coord < total))
    return parts[0][:, None, None] & parts[1][None, :, None] & parts[2][None, None, :]


def harmonic(left, right):
    return 2.0 * left * right / (left + right)


def neighbours(padded):
    return (
        padded[2:, 1:-1, 1:-1],
        padded[:-2, 1:-1, 1:-1],
        padded[1:-1, 2:, 1:-1],
        padded[1:-1, :-2, 1:-1],
        padded[1:-1, 1:-1, 2:],
        padded[1:-1, 1:-1, :-2],
    )


def face_set_zero_outside(cond):
    padded = jnp.pad(cond, 1)
    faces = tuple(harmonic(cond, jnp.where(other > 0.0, other, cond)) for other in neighbours(padded))
    diag = faces[0] + faces[1] + faces[2] + faces[3] + faces[4] + faces[5]
    return faces, diag


def operate(field, faces, diag, scale):
    near = neighbours(jnp.pad(field, 1))
    total = faces[0] * near[0] + faces[1] * near[1] + faces[2] * near[2]
    total = total + faces[3] * near[3] + faces[4] * near[4] + faces[5] * near[5]
    return scale * (diag * field - total)


def smooth(right, start, faces, diag, scale, mask=None):
    def keep(value):
        return value if mask is None else jnp.where(mask, value, 0.0)

    theta = 0.5 * (HIGH + LOW)
    delta = 0.5 * (HIGH - LOW)
    sigma = theta / delta
    rho = 1.0 / sigma
    inverse = 1.0 / (scale * diag)
    if start is None:
        resid = right
        step_dir = inverse * resid / theta
        field = keep(step_dir)
    else:
        resid = right - operate(start, faces, diag, scale)
        step_dir = inverse * resid / theta
        field = keep(start + step_dir)
    for turn in range(DEGREE - 1):
        rho_new = 1.0 / (2.0 * sigma - rho)
        resid = right - operate(field, faces, diag, scale)
        step_dir = rho_new * rho * step_dir + 2.0 * rho_new / delta * inverse * resid
        field = keep(field + step_dir)
        rho = rho_new
    return field


def restrict(field):
    field = field[0::2] + field[1::2]
    field = field[:, 0::2] + field[:, 1::2]
    field = field[:, :, 0::2] + field[:, :, 1::2]
    return field / 8.0


def prolong(field):
    return jnp.repeat(jnp.repeat(jnp.repeat(field, 2, 0), 2, 1), 2, 2)


def centre(field, width):
    return field[width:-width, width:-width, width:-width]


def face_set_global(cond):
    padded = jnp.pad(cond, 1, mode="edge")
    faces = tuple(harmonic(cond, other) for other in neighbours(padded))
    diag = faces[0] + faces[1] + faces[2] + faces[3] + faces[4] + faces[5]
    return faces, diag


def cycle_global(right, cond, level, scale):
    faces, diag = face_set_global(cond)
    if level == LEVELS:
        field = smooth(right, None, faces, diag, scale)
        return smooth(right, field, faces, diag, scale)
    field = smooth(right, None, faces, diag, scale)
    resid = right - operate(field, faces, diag, scale)
    error = cycle_global(restrict(resid), restrict(cond), level + 1, scale * 0.25)
    field = field + prolong(error)
    return smooth(right, field, faces, diag, scale)


def gather_axis(block, axis, dim):
    count = lax.axis_size(axis)
    if count & (count - 1):
        return lax.all_gather(block, axis, axis=dim, tiled=True)
    index = lax.axis_index(axis)
    step = 1
    while step < count:
        theirs = lax.ppermute(block, axis, [(i, i ^ step) for i in range(count)])
        upper = (index // step) % 2 == 1
        low = jnp.where(upper, theirs, block)
        high = jnp.where(upper, block, theirs)
        block = jnp.concatenate([low, high], axis=dim)
        step *= 2
    return block


def gather_global(block):
    block = gather_axis(block, "gz", 3)
    block = gather_axis(block, "gx", 1)
    return gather_axis(block, "gy", 2)


def local(heat_source, material, conductivity):
    cond0 = jnp.zeros(heat_source.shape, jnp.float32)
    for which in range(MATERIALS):
        cond0 = cond0 + jnp.where(material == which, conductivity[which], jnp.float32(0.0))
    cond1 = restrict(cond0)
    cond2 = restrict(cond1)
    cond3 = restrict(cond2)
    block0, block1, block2, block3 = heat_source.shape, cond1.shape, cond2.shape, cond3.shape

    ext0, cond1e, cond2e = exchange(
        [jnp.stack([cond0, heat_source]), cond1, cond2], [HALO0, HALO1, HALO2 + 1]
    )
    cond0e, right0e = ext0[0], ext0[1]

    mask0 = inside_mask(block0, HALO0)
    faces0, diag0 = face_set_zero_outside(cond0e)
    field0 = smooth(right0e, None, faces0, diag0, 1.0, mask0)
    resid0 = centre(right0e - operate(field0, faces0, diag0, 1.0), HALO0)

    faces1, diag1 = face_set_zero_outside(cond1e)
    mask1 = inside_mask(block1, HALO1)
    (right1e,) = exchange([restrict(resid0)], [HALO1])
    field1 = smooth(right1e, None, faces1, diag1, 0.25, mask1)
    resid1 = centre(right1e - operate(field1, faces1, diag1, 0.25), HALO1)

    wide2 = HALO2 + 1
    faces2, diag2 = face_set_zero_outside(cond2e)
    mask2 = inside_mask(block2, wide2)
    (right2e,) = exchange([restrict(resid1)], [HALO2])
    right2e = jnp.pad(right2e, 1)
    field2 = smooth(right2e, None, faces2, diag2, 0.0625, mask2)
    resid2 = centre(right2e - operate(field2, faces2, diag2, 0.0625), wide2)

    whole = gather_global(jnp.stack([cond3, restrict(resid2)]))
    error3 = cycle_global(whole[1], whole[0], 3, 0.015625)

    reach = wide2 // 2 + 1
    padded3 = jnp.pad(error3, reach)
    starts = [lax.axis_index(axis) * n for axis, n in zip(AXES, block3)]
    error3e = lax.dynamic_slice(padded3, starts, [n + 2 * reach for n in block3])
    error3e = centre(prolong(error3e), 2 * reach - wide2)
    field2 = jnp.where(mask2, field2 + error3e, 0.0)
    field2 = smooth(right2e, field2, faces2, diag2, 0.0625, mask2)

    cut = wide2 - HALO1 // 2
    field1 = jnp.where(mask1, field1 + prolong(field2[cut:-cut, cut:-cut, cut:-cut]), 0.0)
    field1 = smooth(right1e, field1, faces1, diag1, 0.25, mask1)

    cut = HALO1 - HALO0 // 2
    error1e = field1[cut:-cut, cut:-cut, cut:-cut]
    field0 = jnp.where(mask0, field0 + prolong(error1e), 0.0)
    field0 = smooth(right0e, field0, faces0, diag0, 1.0, mask0)
    return centre(field0, HALO0)


def solution(mesh):
    in_specs = (P("gx", "gy", "gz"), P("gx", "gy", "gz"), P())
    out_specs = P("gx", "gy", "gz")
    return jax.shard_map(local, mesh=mesh, in_specs=in_specs, out_specs=out_specs, check_vma=False)
```

profile of v0, /device:TPU:10, one launch (start us, length us, event | category | flops | bytes accessed | tf_op | source)
XLA Modules:
  0.0 373.2 jit_solution(11893096267944999483)
XLA Ops:
  1.4 2.8 select_add_fusion
  6.0 3.8 %collective-permute-start.3 = (f32[512]{0:T(512)S(1)}, f32[512]{0:T(512)S(1)}, u32[]{:S(2)}, u32[]{:S(2)}) collective-permute-start(f32[512]{0:T(512)S(1)} %reshape.458), channel_id=1, source_target_pairs={{0,128},{64,192},{128,256},{192,320},{256,384},{320,448},{1,129},{... | collective-permute-start | bytes 6152 | tf_op jit(solution)/shard_map/ppermute | solution.py:45
  11.2 3.6 collective-permute-start.2
  14.9 2.8 fusion.279
  18.6 4.3 %collective-permute-start = (f32[29184]{0:T(1024)S(1)}, f32[29184]{0:T(1024)S(1)}, u32[]{:S(2)}, u32[]{:S(2)}) collective-permute-start(f32[29184]{0:T(1024)S(1)} %get-tuple-element.111), channel_id=1, source_target_pairs={{0,64},{64,128},{128,192},{192,256},{256,320},{320,384},{384,448},... | collective-permute-start | bytes 350216 | tf_op jit(solution)/shard_map/ppermute | solution.py:45
  26.7 4.4 %collective-permute-done.5 = f32[128]{0:T(128)S(1)} collective-permute-done((f32[128]{0:T(128)S(1)}, f32[128]{0:T(128)S(1)}, u32[]{:S(2)}, u32[]{:S(2)}) %collective-permute-start.5) | collective-permute-done | bytes 544 | tf_op jit(solution)/shard_map/ppermute | solution.py:45
  32.3 9.1 %collective-permute-start.6 = (f32[58112]{0:T(1024)S(1)}, f32[58112]{0:T(1024)S(1)}, u32[]{:S(2)}, u32[]{:S(2)}) collective-permute-start(f32[58112]{0:T(1024)S(1)} %get-tuple-element.106), channel_id=1, source_target_pairs={{0,4},{4,8},{8,12},{12,16},{16,20},{20,24},{24,28},{28,32},{32,36}... | collective-permute-start | bytes 697352 | tf_op jit(solution)/shard_map/ppermute | solution.py:45
  41.4 2.8 collective-permute-start.7
  44.3 7.8 %collective-permute-start.8 = (f32[704]{0:T(1024)S(1)}, f32[704]{0:T(1024)S(1)}, u32[]{:S(2)}, u32[]{:S(2)}) collective-permute-start(f32[704]{0:T(1024)S(1)} %reshape.482), channel_id=1, source_target_pairs={{0,12},{4,16},{8,20},{12,24},{16,28},{20,32},{24,36},{28,40},{32,4... | collective-permute-start | bytes 8456 | tf_op jit(solution)/shard_map/ppermute | solution.py:45
  52.1 7.3 %collective-permute-start.9 = (f32[2816]{0:T(1024)S(1)}, f32[2816]{0:T(1024)S(1)}, u32[]{:S(2)}, u32[]{:S(2)}) collective-permute-start(f32[2816]{0:T(1024)S(1)} %reshape.474), channel_id=1, source_target_pairs={{0,8},{4,12},{8,16},{12,20},{16,24},{20,28},{24,32},{28,36},{32,40... | collective-permute-start | bytes 33800 | tf_op jit(solution)/shard_map/ppermute | solution.py:45
  59.4 8.2 %collective-permute-start.10 = (f32[2816]{0:T(1024)S(1)}, f32[2816]{0:T(1024)S(1)}, u32[]{:S(2)}, u32[]{:S(2)}) collective-permute-start(f32[2816]{0:T(1024)S(1)} %reshape.474), channel_id=1, source_target_pairs={{8,0},{12,4},{16,8},{20,12},{24,16},{28,20},{32,24},{36,28},{40,32... | collective-permute-start | bytes 33800 | tf_op jit(solution)/shard_map/ppermute | solution.py:45
  67.7 3.5 collective-permute-done.8
  73.2 7.3 %collective-permute-done.11 = f32[704]{0:T(1024)S(1)} collective-permute-done((f32[704]{0:T(1024)S(1)}, f32[704]{0:T(1024)S(1)}, u32[]{:S(2)}, u32[]{:S(2)}) %collective-permute-start.11) | collective-permute-done | bytes 2848 | tf_op jit(solution)/shard_map/ppermute | solution.py:45
  88.7 3.5 collective-permute-start.12
  95.1 2.7 collective-permute-start.13
  98.2 3.1 collective-permute-done.13
  102.9 2.7 broadcast_multiply_fusion
  119.2 7.9 %collective-permute-start.16 = (f32[12288]{0:T(1024)}, f32[12288]{0:T(1024)S(1)}, u32[]{:S(2)}, u32[]{:S(2)}) collective-permute-start(f32[12288]{0:T(1024)} %reshape.501), channel_id=1, source_target_pairs={{0,4},{4,8},{8,12},{12,16},{16,20},{20,24},{24,28},{28,32},{32,36}... | collective-permute-start | bytes 147464 | tf_op jit(solution)/shard_map/ppermute | solution.py:45
  127.2 2.7 collective-permute-start.17
  131.9 6.3 %collective-permute-done.17 = f32[12288]{0:T(1024)} collective-permute-done((f32[12288]{0:T(1024)}, f32[12288]{0:T(1024)}, u32[]{:S(2)}, u32[]{:S(2)}) %collective-permute-start.17) | collective-permute-done | bytes 49184 | tf_op jit(solution)/shard_map/ppermute | solution.py:45
  142.6 3.2 collective-permute-start.18
  146.5 3.2 collective-permute-start.19
  149.8 3.7 broadcast_multiply_fusion.1
  170.7 4.4 %collective-permute-done.23 = f32[512]{0:T(512)S(1)} collective-permute-done((f32[512]{0:T(512)S(1)}, f32[512]{0:T(512)S(1)}, u32[]{:S(2)}, u32[]{:S(2)}) %collective-permute-start.23) | collective-permute-done | bytes 2080 | tf_op jit(solution)/shard_map/ppermute | solution.py:45
  175.3 21.0 %collective-permute-start.24 = (f32[2560]{0:T(1024)S(1)}, f32[2560]{0:T(1024)S(1)}, u32[]{:S(2)}, u32[]{:S(2)}) collective-permute-start(f32[2560]{0:T(1024)S(1)} %reshape.515), channel_id=1, source_target_pairs={{0,8},{4,12},{8,16},{12,20},{16,24},{20,28},{24,32},{28,36},{32,40... | collective-permute-start | bytes 30728 | tf_op jit(solution)/shard_map/ppermute | solution.py:45
  196.2 3.5 collective-permute-start.25
  199.8 7.1 %collective-permute-start.26 = (f32[2560]{0:T(1024)S(1)}, f32[2560]{0:T(1024)}, u32[]{:S(2)}, u32[]{:S(2)}) collective-permute-start(f32[2560]{0:T(1024)S(1)} %reshape.515), channel_id=1, source_target_pairs={{4,0},{8,4},{12,8},{16,12},{20,16},{24,20},{28,24},{32,28},{36,32}... | collective-permute-start | bytes 30728 | tf_op jit(solution)/shard_map/ppermute | solution.py:45
  206.9 4.5 %collective-permute-start.27 = (f32[2560]{0:T(1024)S(1)}, f32[2560]{0:T(1024)S(1)}, u32[]{:S(2)}, u32[]{:S(2)}) collective-permute-start(f32[2560]{0:T(1024)S(1)} %reshape.515), channel_id=1, source_target_pairs={{8,0},{12,4},{16,8},{20,12},{24,16},{28,20},{32,24},{36,28},{40,32... | collective-permute-start | bytes 30728 | tf_op jit(solution)/shard_map/ppermute | solution.py:45
  214.4 6.8 %collective-permute-done.27 = f32[2560]{0:T(1024)S(1)} collective-permute-done((f32[2560]{0:T(1024)S(1)}, f32[2560]{0:T(1024)S(1)}, u32[]{:S(2)}, u32[]{:S(2)}) %collective-permute-start.27) | collective-permute-done | bytes 10272 | tf_op jit(solution)/shard_map/ppermute | solution.py:45
  221.9 2.8 concatenate.137
  231.4 3.2 collective-permute-start.29
  234.6 3.8 %broadcast_multiply_fusion.2 = (f32[22,22,50]{2,1,0:T(8,128)}, f32[22,22,50]{2,1,0:T(8,128)}, f32[22,22,50]{2,1,0:T(8,128)}, f32[22,22,50]{2,1,0:T(8,128)}, f32[...) fusion(f32[22,22,50]{2,1,0:T(8,128)} %pad_maximum_fusion.12), kind=kLoop, calls=%fused_computation.484 | loop fusion | flops 943800 | bytes 871200 | tf_op jit(solution)/shard_map/mul | solution.py:118
  247.2 3.6 collective-permute-done.30
  250.9 2.6 collective-permute-start.31
  253.5 4.3 %collective-permute-done.31 = f32[2,2,2,32]{3,2,1,0:T(2,128)S(1)} collective-permute-done((f32[2,2,2,32]{3,2,1,0:T(2,128)S(1)}, f32[2,2,2,32]{3,2,1,0:T(2,128)S(1)}, u32[]{:S(2)}, u32[]{:S(2)}) %collective-permute-start.31) | collective-permute-done | bytes 1056 | tf_op jit(solution)/shard_map/ppermute | solution.py:165
  261.2 3.9 %collective-permute-start.33 = (f32[2,4,2,64]{3,2,1,0:T(2,128)S(1)}, f32[2,4,2,64]{3,2,1,0:T(2,128)S(1)}, u32[]{:S(2)}, u32[]{:S(2)}) collective-permute-start(f32[2,4,2,64]{3,2,1,0:T(2,128)S(1)} %pad_maximum_fusion.48), channel_id=1, source_target_pairs={{0,128},{64,192},{128,0},{192,64},{256,384},{320,448},{384,256},{4... | collective-permute-start | bytes 12296 | tf_op jit(solution)/shard_map/ppermute | solution.py:165
  266.7 3.6 collective-permute-start.34
  270.4 2.9 collective-permute-done.34
  273.3 2.6 collective-permute-start.35
  276.0 7.1 %collective-permute-done.35 = f32[2,16,2,64]{3,2,1,0:T(2,128)S(1)} collective-permute-done((f32[2,16,2,64]{3,2,1,0:T(2,128)S(1)}, f32[2,16,2,64]{3,2,1,0:T(2,128)S(1)}, u32[]{:S(2)}, u32[]{:S(2)}) %collective-permute-start.35) | collective-permute-done | bytes 16416 | tf_op jit(solution)/shard_map/ppermute | solution.py:165
  283.1 5.2 %collective-permute-start.36 = (f32[2,16,4,64]{3,2,1,0:T(4,128)S(1)}, f32[2,16,4,64]{3,2,1,0:T(4,128)}, u32[]{:S(2)}, u32[]{:S(2)}) collective-permute-start(f32[2,16,4,64]{3,2,1,0:T(4,128)S(1)} %pad_maximum_fusion.42), channel_id=1, source_target_pairs={{0,8},{4,12},{8,0},{12,4},{16,24},{20,28},{24,16},{28,20},{32,40},... | collective-permute-start | bytes 98312 | tf_op jit(solution)/shard_map/ppermute | solution.py:165
  289.3 10.5 %collective-permute-done.36 = f32[2,16,4,64]{3,2,1,0:T(4,128)} collective-permute-done((f32[2,16,4,64]{3,2,1,0:T(4,128)S(1)}, f32[2,16,4,64]{3,2,1,0:T(4,128)}, u32[]{:S(2)}, u32[]{:S(2)}) %collective-permute-start.36) | collective-permute-done | bytes 32800 | tf_op jit(solution)/shard_map/ppermute | solution.py:165
  304.6 4.0 %collective-permute-done.37 = f32[2,16,8,64]{3,2,1,0:T(8,128)} collective-permute-done((f32[2,16,8,64]{3,2,1,0:T(8,128)}, f32[2,16,8,64]{3,2,1,0:T(8,128)}, u32[]{:S(2)}, u32[]{:S(2)}) %collective-permute-start.37) | collective-permute-done | bytes 65568 | tf_op jit(solution)/shard_map/ppermute | solution.py:165
  312.2 7.1 %collective-permute-done.38 = f32[2,16,16,64]{3,2,1,0:T(8,128)S(1)} collective-permute-done((f32[2,16,16,64]{3,2,1,0:T(8,128)S(1)}, f32[2,16,16,64]{3,2,1,0:T(8,128)S(1)}, u32[]{:S(2)}, u32[]{:S(2)}) %collective-permute-start.38) | collective-permute-done | bytes 131104 | tf_op jit(solution)/shard_map/ppermute | solution.py:165
  351.7 3.2 broadcast_in_dim.88
  354.9 3.6 reshape.532
  358.6 3.5 copy.21
  364.4 3.2 and_select_fusion.1
  (420 shorter events, 136.0 us)
Async XLA Ops:
  0.0 32.1 %copy-start.42 = (f32[16,16,128]{2,1,0:T(8,128)S(1)}, f32[16,16,128]{2,1,0:T(8,128)}, u32[]{:S(2)}) copy-start(f32[16,16,128]{2,1,0:T(8,128)} %param.3) | copy-start | bytes 393220
  6.0 25.2 %collective-permute-start.3 = (f32[512]{0:T(512)S(1)}, f32[512]{0:T(512)S(1)}, u32[]{:S(2)}, u32[]{:S(2)}) collective-permute-start(f32[512]{0:T(512)S(1)} %reshape.458), channel_id=1, source_target_pairs={{0,128},{64,192},{128,256},{192,320},{256,384},{320,448},{1,129},{... | collective-permute-start | bytes 6152 | tf_op jit(solution)/shard_map/ppermute | solution.py:45
  9.8 21.4 %collective-permute-start.4 = (f32[512]{0:T(512)S(1)}, f32[512]{0:T(512)S(1)}, u32[]{:S(2)}, u32[]{:S(2)}) collective-permute-start(f32[512]{0:T(512)S(1)} %reshape.458), channel_id=1, source_target_pairs={{128,0},{192,64},{256,128},{320,192},{384,256},{448,320},{129,1},{... | collective-permute-start | bytes 6152 | tf_op jit(solution)/shard_map/ppermute | solution.py:45
  11.2 14.1 %collective-permute-start.2 = (f32[128]{0:T(128)S(1)}, f32[128]{0:T(128)S(1)}, u32[]{:S(2)}, u32[]{:S(2)}) collective-permute-start(f32[128]{0:T(128)S(1)} %reshape.466), channel_id=1, source_target_pairs={{0,192},{64,256},{128,320},{192,384},{256,448},{1,193},{65,257},{1... | collective-permute-start | bytes 1544 | tf_op jit(solution)/shard_map/ppermute | solution.py:45
  18.6 12.8 %collective-permute-start = (f32[29184]{0:T(1024)S(1)}, f32[29184]{0:T(1024)S(1)}, u32[]{:S(2)}, u32[]{:S(2)}) collective-permute-start(f32[29184]{0:T(1024)S(1)} %get-tuple-element.111), channel_id=1, source_target_pairs={{0,64},{64,128},{128,192},{192,256},{256,320},{320,384},{384,448},... | collective-permute-start | bytes 350216 | tf_op jit(solution)/shard_map/ppermute | solution.py:45
  22.9 8.5 %collective-permute-start.1 = (f32[29184]{0:T(1024)S(1)}, f32[29184]{0:T(1024)S(1)}, u32[]{:S(2)}, u32[]{:S(2)}) collective-permute-start(f32[29184]{0:T(1024)S(1)} %get-tuple-element.110), channel_id=1, source_target_pairs={{64,0},{128,64},{192,128},{256,192},{320,256},{384,320},{448,384},... | collective-permute-start | bytes 350216 | tf_op jit(solution)/shard_map/ppermute | solution.py:45
  25.4 5.8 %collective-permute-start.5 = (f32[128]{0:T(128)S(1)}, f32[128]{0:T(128)S(1)}, u32[]{:S(2)}, u32[]{:S(2)}) collective-permute-start(f32[128]{0:T(128)S(1)} %reshape.472), channel_id=1, source_target_pairs={{192,0},{256,64},{320,128},{384,192},{448,256},{193,1},{257,65},{3... | collective-permute-start | bytes 1544 | tf_op jit(solution)/shard_map/ppermute | solution.py:45
  31.9 51.5 %copy-start.51 = (f32[8,8,64]{2,1,0:T(8,128)}, f32[8,8,64]{2,1,0:T(8,128)S(1)}, u32[]{:S(2)}) copy-start(f32[8,8,64]{2,1,0:T(8,128)S(1)} %reshape.463) | copy-start | bytes 49156
  31.9 51.4 %copy-start.53 = (f32[8,8,64]{2,1,0:T(8,128)}, f32[8,8,64]{2,1,0:T(8,128)S(1)}, u32[]{:S(2)}) copy-start(f32[8,8,64]{2,1,0:T(8,128)S(1)} %reshape.464) | copy-start | bytes 49156
  32.3 48.6 %collective-permute-start.6 = (f32[58112]{0:T(1024)S(1)}, f32[58112]{0:T(1024)S(1)}, u32[]{:S(2)}, u32[]{:S(2)}) collective-permute-start(f32[58112]{0:T(1024)S(1)} %get-tuple-element.106), channel_id=1, source_target_pairs={{0,4},{4,8},{8,12},{12,16},{16,20},{20,24},{24,28},{28,32},{32,36}... | collective-permute-start | bytes 697352 | tf_op jit(solution)/shard_map/ppermute | solution.py:45
  41.4 39.6 %collective-permute-start.7 = (f32[58112]{0:T(1024)S(1)}, f32[58112]{0:T(1024)S(1)}, u32[]{:S(2)}, u32[]{:S(2)}) collective-permute-start(f32[58112]{0:T(1024)S(1)} %get-tuple-element.107), channel_id=1, source_target_pairs={{4,0},{8,4},{12,8},{16,12},{20,16},{24,20},{28,24},{32,28},{36,32}... | collective-permute-start | bytes 697352 | tf_op jit(solution)/shard_map/ppermute | solution.py:45
  44.3 26.9 %collective-permute-start.8 = (f32[704]{0:T(1024)S(1)}, f32[704]{0:T(1024)S(1)}, u32[]{:S(2)}, u32[]{:S(2)}) collective-permute-start(f32[704]{0:T(1024)S(1)} %reshape.482), channel_id=1, source_target_pairs={{0,12},{4,16},{8,20},{12,24},{16,28},{20,32},{24,36},{28,40},{32,4... | collective-permute-start | bytes 8456 | tf_op jit(solution)/shard_map/ppermute | solution.py:45
  52.1 28.5 %collective-permute-start.9 = (f32[2816]{0:T(1024)S(1)}, f32[2816]{0:T(1024)S(1)}, u32[]{:S(2)}, u32[]{:S(2)}) collective-permute-start(f32[2816]{0:T(1024)S(1)} %reshape.474), channel_id=1, source_target_pairs={{0,8},{4,12},{8,16},{12,20},{16,24},{20,28},{24,32},{28,36},{32,40... | collective-permute-start | bytes 33800 | tf_op jit(solution)/shard_map/ppermute | solution.py:45
  59.4 21.3 %collective-permute-start.10 = (f32[2816]{0:T(1024)S(1)}, f32[2816]{0:T(1024)S(1)}, u32[]{:S(2)}, u32[]{:S(2)}) collective-permute-start(f32[2816]{0:T(1024)S(1)} %reshape.474), channel_id=1, source_target_pairs={{8,0},{12,4},{16,8},{20,12},{24,16},{28,20},{32,24},{36,28},{40,32... | collective-permute-start | bytes 33800 | tf_op jit(solution)/shard_map/ppermute | solution.py:45
  71.2 9.4 %collective-permute-start.11 = (f32[704]{0:T(1024)S(1)}, f32[704]{0:T(1024)S(1)}, u32[]{:S(2)}, u32[]{:S(2)}) collective-permute-start(f32[704]{0:T(1024)S(1)} %reshape.488), channel_id=1, source_target_pairs={{12,0},{16,4},{20,8},{24,12},{28,16},{32,20},{36,24},{40,28},{44,3... | collective-permute-start | bytes 8456 | tf_op jit(solution)/shard_map/ppermute | solution.py:45
  88.7 9.1 %collective-permute-start.12 = (f32[18372]{0:T(1024)S(1)}, f32[18372]{0:T(1024)S(1)}, u32[]{:S(2)}, u32[]{:S(2)}) collective-permute-start(f32[18372]{0:T(1024)S(1)} %concatenate.128), channel_id=1, source_target_pairs={{0,1},{1,2},{2,3},{4,5},{5,6},{6,7},{8,9},{9,10},{10,11},{12,13},{... | collective-permute-start | bytes 220472 | tf_op jit(solution)/shard_map/ppermute | solution.py:45
  95.1 6.2 %collective-permute-start.13 = (f32[18372]{0:T(1024)S(1)}, f32[18372]{0:T(1024)S(1)}, u32[]{:S(2)}, u32[]{:S(2)}) collective-permute-start(f32[18372]{0:T(1024)S(1)} %concatenate.129), channel_id=1, source_target_pairs={{1,0},{2,1},{3,2},{5,4},{6,5},{7,6},{9,8},{10,9},{11,10},{13,12},{... | collective-permute-start | bytes 220472 | tf_op jit(solution)/shard_map/ppermute | solution.py:45
  110.6 19.2 %copy-start.47 = (f32[24,8,64]{2,1,0:T(8,128)S(1)}, f32[24,8,64]{2,1,0:T(8,128)}, u32[]{:S(2)}) copy-start(f32[24,8,64]{2,1,0:T(8,128)} %copy-done.46) | copy-start | bytes 147460
  110.7 19.2 %copy-start.49 = (f32[24,8,64]{2,1,0:T(8,128)S(1)}, f32[24,8,64]{2,1,0:T(8,128)}, u32[]{:S(2)}) copy-start(f32[24,8,64]{2,1,0:T(8,128)} %copy-done.48) | copy-start | bytes 147460
  110.7 19.2 %copy-start.52 = (f32[8,8,64]{2,1,0:T(8,128)S(1)}, f32[8,8,64]{2,1,0:T(8,128)}, u32[]{:S(2)}) copy-start(f32[8,8,64]{2,1,0:T(8,128)} %copy-done.51) | copy-start | bytes 49156
  110.7 19.2 %copy-start.54 = (f32[8,8,64]{2,1,0:T(8,128)S(1)}, f32[8,8,64]{2,1,0:T(8,128)}, u32[]{:S(2)}) copy-start(f32[8,8,64]{2,1,0:T(8,128)} %copy-done.53) | copy-start | bytes 49156
  112.5 26.7 %copy-start.50 = (f32[8,8,64]{2,1,0:T(8,128)}, f32[8,8,64]{2,1,0:T(8,128)S(1)}, u32[]{:S(2)}) copy-start(f32[8,8,64]{2,1,0:T(8,128)S(1)} %add_multiply_fusion) | copy-start | bytes 49156
  112.6 5.8 %collective-permute-start.14 = (f32[4096]{0:T(1024)S(1)}, f32[4096]{0:T(1024)S(1)}, u32[]{:S(2)}, u32[]{:S(2)}) collective-permute-start(f32[4096]{0:T(1024)S(1)} %reshape.498), channel_id=1, source_target_pairs={{0,64},{64,128},{128,192},{192,256},{256,320},{320,384},{384,448},... | collective-permute-start | bytes 49160 | tf_op jit(solution)/shard_map/ppermute | solution.py:45
  113.9 4.6 %collective-permute-start.15 = (f32[4096]{0:T(1024)S(1)}, f32[4096]{0:T(1024)S(1)}, u32[]{:S(2)}, u32[]{:S(2)}) collective-permute-start(f32[4096]{0:T(1024)S(1)} %reshape.498), channel_id=1, source_target_pairs={{64,0},{128,64},{192,128},{256,192},{320,256},{384,320},{448,384},... | collective-permute-start | bytes 49160 | tf_op jit(solution)/shard_map/ppermute | solution.py:45
  119.2 12.6 %collective-permute-start.16 = (f32[12288]{0:T(1024)}, f32[12288]{0:T(1024)S(1)}, u32[]{:S(2)}, u32[]{:S(2)}) collective-permute-start(f32[12288]{0:T(1024)} %reshape.501), channel_id=1, source_target_pairs={{0,4},{4,8},{8,12},{12,16},{16,20},{20,24},{24,28},{28,32},{32,36}... | collective-permute-start | bytes 147464 | tf_op jit(solution)/shard_map/ppermute | solution.py:45
  127.2 11.1 %collective-permute-start.17 = (f32[12288]{0:T(1024)}, f32[12288]{0:T(1024)}, u32[]{:S(2)}, u32[]{:S(2)}) collective-permute-start(f32[12288]{0:T(1024)} %reshape.501), channel_id=1, source_target_pairs={{4,0},{8,4},{12,8},{16,12},{20,16},{24,20},{28,24},{32,28},{36,32}... | collective-permute-start | bytes 147464 | tf_op jit(solution)/shard_map/ppermute | solution.py:45
  142.6 10.9 %collective-permute-start.18 = (f32[4608]{0:T(1024)}, f32[4608]{0:T(1024)}, u32[]{:S(2)}, u32[]{:S(2)}) collective-permute-start(f32[4608]{0:T(1024)} %reshape.504), channel_id=1, source_target_pairs={{0,1},{1,2},{2,3},{4,5},{5,6},{6,7},{8,9},{9,10},{10,11},{12,13},{... | collective-permute-start | bytes 55304 | tf_op jit(solution)/shard_map/ppermute | solution.py:45
  146.5 8.5 %collective-permute-start.19 = (f32[4608]{0:T(1024)}, f32[4608]{0:T(1024)}, u32[]{:S(2)}, u32[]{:S(2)}) collective-permute-start(f32[4608]{0:T(1024)} %reshape.506), channel_id=1, source_target_pairs={{1,0},{2,1},{3,2},{5,4},{6,5},{7,6},{9,8},{10,9},{11,10},{13,12},{... | collective-permute-start | bytes 55304 | tf_op jit(solution)/shard_map/ppermute | solution.py:45
  161.1 8.8 %collective-permute-start.20 = (f32[512]{0:T(512)S(1)}, f32[512]{0:T(512)S(1)}, u32[]{:S(2)}, u32[]{:S(2)}) collective-permute-start(f32[512]{0:T(512)S(1)} %reshape.510), channel_id=1, source_target_pairs={{0,128},{64,192},{128,256},{192,320},{256,384},{320,448},{1,129},{... | collective-permute-start | bytes 6152 | tf_op jit(solution)/shard_map/ppermute | solution.py:45
  162.6 81.2 %copy-start.62 = (pred[50]{0:T(512)(128)(4,1)}, pred[50]{0:T(512)(128)(4,1)S(1)}, u32[]{:S(2)}) copy-start(pred[50]{0:T(512)(128)(4,1)S(1)} %compare_and_fusion) | copy-start | bytes 154
  166.0 4.0 %collective-permute-start.21 = (f32[512]{0:T(512)S(1)}, f32[512]{0:T(512)S(1)}, u32[]{:S(2)}, u32[]{:S(2)}) collective-permute-start(f32[512]{0:T(512)S(1)} %reshape.510), channel_id=1, source_target_pairs={{0,64},{64,128},{128,192},{192,256},{256,320},{320,384},{384,448},... | collective-permute-start | bytes 6152 | tf_op jit(solution)/shard_map/ppermute | solution.py:45
  167.3 3.3 collective-permute-start.22
  168.6 6.5 %collective-permute-start.23 = (f32[512]{0:T(512)S(1)}, f32[512]{0:T(512)S(1)}, u32[]{:S(2)}, u32[]{:S(2)}) collective-permute-start(f32[512]{0:T(512)S(1)} %reshape.510), channel_id=1, source_target_pairs={{128,0},{192,64},{256,128},{320,192},{384,256},{448,320},{129,1},{... | collective-permute-start | bytes 6152 | tf_op jit(solution)/shard_map/ppermute | solution.py:45
  175.3 38.2 %collective-permute-start.24 = (f32[2560]{0:T(1024)S(1)}, f32[2560]{0:T(1024)S(1)}, u32[]{:S(2)}, u32[]{:S(2)}) collective-permute-start(f32[2560]{0:T(1024)S(1)} %reshape.515), channel_id=1, source_target_pairs={{0,8},{4,12},{8,16},{12,20},{16,24},{20,28},{24,32},{28,36},{32,40... | collective-permute-start | bytes 30728 | tf_op jit(solution)/shard_map/ppermute | solution.py:45
  196.2 17.3 %collective-permute-start.25 = (f32[2560]{0:T(1024)S(1)}, f32[2560]{0:T(1024)S(1)}, u32[]{:S(2)}, u32[]{:S(2)}) collective-permute-start(f32[2560]{0:T(1024)S(1)} %reshape.515), channel_id=1, source_target_pairs={{0,4},{4,8},{8,12},{12,16},{16,20},{20,24},{24,28},{28,32},{32,36}... | collective-permute-start | bytes 30728 | tf_op jit(solution)/shard_map/ppermute | solution.py:45
  199.8 13.9 %collective-permute-start.26 = (f32[2560]{0:T(1024)S(1)}, f32[2560]{0:T(1024)}, u32[]{:S(2)}, u32[]{:S(2)}) collective-permute-start(f32[2560]{0:T(1024)S(1)} %reshape.515), channel_id=1, source_target_pairs={{4,0},{8,4},{12,8},{16,12},{20,16},{24,20},{28,24},{32,28},{36,32}... | collective-permute-start | bytes 30728 | tf_op jit(solution)/shard_map/ppermute | solution.py:45
  206.9 14.3 %collective-permute-start.27 = (f32[2560]{0:T(1024)S(1)}, f32[2560]{0:T(1024)S(1)}, u32[]{:S(2)}, u32[]{:S(2)}) collective-permute-start(f32[2560]{0:T(1024)S(1)} %reshape.515), channel_id=1, source_target_pairs={{8,0},{12,4},{16,8},{20,12},{24,16},{28,20},{32,24},{36,28},{40,32... | collective-permute-start | bytes 30728 | tf_op jit(solution)/shard_map/ppermute | solution.py:45
  227.7 10.7 %collective-permute-start.28 = (f32[3200]{0:T(1024)S(1)}, f32[3200]{0:T(1024)S(1)}, u32[]{:S(2)}, u32[]{:S(2)}) collective-permute-start(f32[3200]{0:T(1024)S(1)} %reshape.520), channel_id=1, source_target_pairs={{0,1},{1,2},{2,3},{4,5},{5,6},{6,7},{8,9},{9,10},{10,11},{12,13},{... | collective-permute-start | bytes 38408 | tf_op jit(solution)/shard_map/ppermute | solution.py:45
  231.4 7.9 %collective-permute-start.29 = (f32[3200]{0:T(1024)S(1)}, f32[3200]{0:T(1024)S(1)}, u32[]{:S(2)}, u32[]{:S(2)}) collective-permute-start(f32[3200]{0:T(1024)S(1)} %reshape.522), channel_id=1, source_target_pairs={{1,0},{2,1},{3,2},{5,4},{6,5},{7,6},{9,8},{10,9},{11,10},{13,12},{... | collective-permute-start | bytes 38408 | tf_op jit(solution)/shard_map/ppermute | solution.py:45
  245.3 5.5 %collective-permute-start.30 = (f32[2,2,2,16]{3,2,1,0:T(2,128)S(1)}, f32[2,2,2,16]{3,2,1,0:T(2,128)S(1)}, u32[]{:S(2)}, u32[]{:S(2)}) collective-permute-start(f32[2,2,2,16]{3,2,1,0:T(2,128)S(1)} %pad_maximum_fusion.49), channel_id=1, source_target_pairs={{0,1},{1,0},{2,3},{3,2},{4,5},{5,4},{6,7},{7,6},{8,9},{9,8},{10,11... | collective-permute-start | bytes 1544 | tf_op jit(solution)/shard_map/ppermute | solution.py:165
  250.9 7.0 %collective-permute-start.31 = (f32[2,2,2,32]{3,2,1,0:T(2,128)S(1)}, f32[2,2,2,32]{3,2,1,0:T(2,128)S(1)}, u32[]{:S(2)}, u32[]{:S(2)}) collective-permute-start(f32[2,2,2,32]{3,2,1,0:T(2,128)S(1)} %pad_maximum_fusion.50), channel_id=1, source_target_pairs={{0,2},{1,3},{2,0},{3,1},{4,6},{5,7},{6,4},{7,5},{8,10},{9,11},{10,... | collective-permute-start | bytes 3080 | tf_op jit(solution)/shard_map/ppermute | solution.py:165
  258.0 3.0 collective-permute-start.32
  261.2 5.5 %collective-permute-start.33 = (f32[2,4,2,64]{3,2,1,0:T(2,128)S(1)}, f32[2,4,2,64]{3,2,1,0:T(2,128)S(1)}, u32[]{:S(2)}, u32[]{:S(2)}) collective-permute-start(f32[2,4,2,64]{3,2,1,0:T(2,128)S(1)} %pad_maximum_fusion.48), channel_id=1, source_target_pairs={{0,128},{64,192},{128,0},{192,64},{256,384},{320,448},{384,256},{4... | collective-permute-start | bytes 12296 | tf_op jit(solution)/shard_map/ppermute | solution.py:165
  266.7 6.5 %collective-permute-start.34 = (f32[2,8,2,64]{3,2,1,0:T(2,128)S(1)}, f32[2,8,2,64]{3,2,1,0:T(2,128)S(1)}, u32[]{:S(2)}, u32[]{:S(2)}) collective-permute-start(f32[2,8,2,64]{3,2,1,0:T(2,128)S(1)} %pad_maximum_fusion.44), channel_id=1, source_target_pairs={{0,256},{64,320},{128,384},{192,448},{256,0},{320,64},{384,128},{4... | collective-permute-start | bytes 24584 | tf_op jit(solution)/shard_map/ppermute | solution.py:165
  273.3 9.7 %collective-permute-start.35 = (f32[2,16,2,64]{3,2,1,0:T(2,128)S(1)}, f32[2,16,2,64]{3,2,1,0:T(2,128)S(1)}, u32[]{:S(2)}, u32[]{:S(2)}) collective-permute-start(f32[2,16,2,64]{3,2,1,0:T(2,128)S(1)} %pad_maximum_fusion.43), channel_id=1, source_target_pairs={{0,4},{4,0},{8,12},{12,8},{16,20},{20,16},{24,28},{28,24},{32,36},... | collective-permute-start | bytes 49160 | tf_op jit(solution)/shard_map/ppermute | solution.py:165
  283.1 16.6 %collective-permute-start.36 = (f32[2,16,4,64]{3,2,1,0:T(4,128)S(1)}, f32[2,16,4,64]{3,2,1,0:T(4,128)}, u32[]{:S(2)}, u32[]{:S(2)}) collective-permute-start(f32[2,16,4,64]{3,2,1,0:T(4,128)S(1)} %pad_maximum_fusion.42), channel_id=1, source_target_pairs={{0,8},{4,12},{8,0},{12,4},{16,24},{20,28},{24,16},{28,20},{32,40},... | collective-permute-start | bytes 98312 | tf_op jit(solution)/shard_map/ppermute | solution.py:165
  301.3 7.2 %collective-permute-start.37 = (f32[2,16,8,64]{3,2,1,0:T(8,128)}, f32[2,16,8,64]{3,2,1,0:T(8,128)}, u32[]{:S(2)}, u32[]{:S(2)}) collective-permute-start(f32[2,16,8,64]{3,2,1,0:T(8,128)} %pad_maximum_fusion.37), channel_id=1, source_target_pairs={{0,16},{4,20},{8,24},{12,28},{16,0},{20,4},{24,8},{28,12},{32,48},... | collective-permute-start | bytes 196616 | tf_op jit(solution)/shard_map/ppermute | solution.py:165
  309.6 9.8 %collective-permute-start.38 = (f32[2,16,16,64]{3,2,1,0:T(8,128)S(1)}, f32[2,16,16,64]{3,2,1,0:T(8,128)S(1)}, u32[]{:S(2)}, u32[]{:S(2)}) collective-permute-start(f32[2,16,16,64]{3,2,1,0:T(8,128)S(1)} %pad_maximum_fusion.32), channel_id=1, source_target_pairs={{0,32},{4,36},{8,40},{12,44},{16,48},{20,52},{24,56},{28,60},{32,0... | collective-permute-start | bytes 393224 | tf_op jit(solution)/shard_map/ppermute | solution.py:165
  (56 other events, 180.0 us)
where the time goes:
time: 381 us; the launch traced here: 373 us
  starting transfers between devices  152 us (40%)
  waiting for transfers between devices  78.4 us (21%)
  local copies, waits for them, and re-layouts  73 us (19%)
  other arithmetic  67.9 us (18%)
    ppermute x30, starting transfers between devices, exchange(): flat = lax.ppermute(flat, axis, pairs)  126 us
    ppermute x9, waiting for transfers between devices, gather_axis(): theirs = lax.ppermute(block, axis, [(i, i ^ step) for i in range(count)])  42.1 us
    ppermute x30, waiting for transfers between devices, exchange(): flat = lax.ppermute(flat, axis, pairs)  36.3 us
    ppermute x9, starting transfers between devices, gather_axis(): theirs = lax.ppermute(block, axis, [(i, i ^ step) for i in range(count)])  25.7 us
    select_n x16, other arithmetic, keep(): return value if mask is None else jnp.where(mask, value, 0.0)  22.9 us
    reshape x7, local copies, waits for them, and re-layouts, prolong(): return jnp.repeat(jnp.repeat(jnp.repeat(field, 2, 0), 2, 1), 2, 2)  16 us
    reshape x40, local copies, waits for them, and re-layouts, exchange(): got.append(flat[at:at + s.size].reshape(s.shape))  12.9 us
    reshape x24, local copies, waits for them, and re-layouts, exchange(): flat = jnp.concatenate([s.reshape(-1) for s in slabs])  11 us
  transfers between devices with their start and end apart: 39, of which 17 were waited for; matrix products, arithmetic and copies ran while one was open for 10% of the time, Pallas kernels for 0%

commit v1 on v0

--- a/solution.py
+++ b/solution.py
@@ -14,6 +14,7 @@
 HALO0 = 6
 HALO1 = 8
 HALO2 = 8
+BUTTERFLY = False
 
 
 def exchange(blocks, widths):
@@ -157,7 +158,7 @@
 
 def gather_axis(block, axis, dim):
     count = lax.axis_size(axis)
-    if count & (count - 1):
+    if count & (count - 1) or not BUTTERFLY:
         return lax.all_gather(block, axis, axis=dim, tiled=True)
     index = lax.axis_index(axis)
     step = 1

time: 381 us -> 390 us (1.024)
  the two profiles are of different devices: /device:TPU:10 before, /device:TPU:38 now
where the time goes in v1:
time: 390 us; the launch traced here: 383 us
  starting transfers between devices  134 us (34%)
  blocking collectives  83.8 us (21%)
  local copies, waits for them, and re-layouts  77.6 us (20%)
  other arithmetic  65.5 us (17%)
  waiting for transfers between devices  19.8 us (5%)
    ppermute x30, starting transfers between devices, exchange(): flat = lax.ppermute(flat, axis, pairs)  134 us
    all_gather x3, blocking collectives, gather_axis(): return lax.all_gather(block, axis, axis=dim, tiled=True)  83.8 us
    select_n x16, other arithmetic, keep(): return value if mask is None else jnp.where(mask, value, 0.0)  23 us
    ppermute x30, waiting for transfers between devices, exchange(): flat = lax.ppermute(flat, axis, pairs)  19.8 us
    reshape x40, local copies, waits for them, and re-layouts, exchange(): got.append(flat[at:at + s.size].reshape(s.shape))  16.3 us
    reshape x7, local copies, waits for them, and re-layouts, prolong(): return jnp.repeat(jnp.repeat(jnp.repeat(field, 2, 0), 2, 1), 2, 2)  16 us
    reshape x24, local copies, waits for them, and re-layouts, exchange(): flat = jnp.concatenate([s.reshape(-1) for s in slabs])  11.6 us
    mul x3, other arithmetic, smooth(): 2.0 * rho_new / delta * inverse * resid  10.3 us
  transfers between devices with their start and end apart: 30, of which 6 were waited for; matrix products, arithmetic and copies ran while one was open for 10% of the time, Pallas kernels for 0%

profile of v1, /device:TPU:38, one launch (start us, length us, event | category | flops | bytes accessed | tf_op | source)
XLA Modules:
  0.0 382.9 jit_solution(12390739153028701842)
XLA Ops:
  1.4 2.8 select_add_fusion
  6.0 3.8 collective-permute-start.3
  9.8 2.0 collective-permute-start.4
  11.9 2.8 fusion.267
  17.5 3.6 collective-permute-start.1
  21.3 3.7 collective-permute-start.2
  28.4 3.5 collective-permute-done.5
  33.0 9.1 %collective-permute-start.6 = (f32[58112]{0:T(1024)S(1)}, f32[58112]{0:T(1024)S(1)}, u32[]{:S(2)}, u32[]{:S(2)}) collective-permute-start(f32[58112]{0:T(1024)S(1)} %get-tuple-element.97), channel_id=1, source_target_pairs={{0,4},{4,8},{8,12},{12,16},{16,20},{20,24},{24,28},{28,32},{32,36}... | collective-permute-start | bytes 697352 | tf_op jit(solution)/shard_map/ppermute | solution.py:46
  42.1 3.1 collective-permute-start.7
  45.3 7.6 %collective-permute-start.8 = (f32[704]{0:T(1024)S(1)}, f32[704]{0:T(1024)S(1)}, u32[]{:S(2)}, u32[]{:S(2)}) collective-permute-start(f32[704]{0:T(1024)S(1)} %reshape.482), channel_id=1, source_target_pairs={{0,12},{4,16},{8,20},{12,24},{16,28},{20,32},{24,36},{28,40},{32,4... | collective-permute-start | bytes 8456 | tf_op jit(solution)/shard_map/ppermute | solution.py:46
  53.0 4.3 %collective-permute-start.9 = (f32[2816]{0:T(1024)S(1)}, f32[2816]{0:T(1024)S(1)}, u32[]{:S(2)}, u32[]{:S(2)}) collective-permute-start(f32[2816]{0:T(1024)S(1)} %reshape.474), channel_id=1, source_target_pairs={{0,8},{4,12},{8,16},{12,20},{16,24},{20,28},{24,32},{28,36},{32,40... | collective-permute-start | bytes 33800 | tf_op jit(solution)/shard_map/ppermute | solution.py:46
  57.2 11.2 %collective-permute-start.10 = (f32[2816]{0:T(1024)S(1)}, f32[2816]{0:T(1024)S(1)}, u32[]{:S(2)}, u32[]{:S(2)}) collective-permute-start(f32[2816]{0:T(1024)S(1)} %reshape.474), channel_id=1, source_target_pairs={{8,0},{12,4},{16,8},{20,12},{24,16},{28,20},{32,24},{36,28},{40,32... | collective-permute-start | bytes 33800 | tf_op jit(solution)/shard_map/ppermute | solution.py:46
  68.5 3.1 collective-permute-start.11
  72.2 5.7 %collective-permute-done.11 = f32[704]{0:T(1024)S(1)} collective-permute-done((f32[704]{0:T(1024)S(1)}, f32[704]{0:T(1024)S(1)}, u32[]{:S(2)}, u32[]{:S(2)}) %collective-permute-start.11) | collective-permute-done | bytes 2848 | tf_op jit(solution)/shard_map/ppermute | solution.py:46
  85.4 3.5 collective-permute-start.12
  94.5 3.5 collective-permute-done.13
  99.6 2.7 broadcast_multiply_fusion
  111.8 3.6 collective-permute-start.15
  127.9 8.7 %collective-permute-start.17 = (f32[12288]{0:T(1024)}, f32[12288]{0:T(1024)}, u32[]{:S(2)}, u32[]{:S(2)}) collective-permute-start(f32[12288]{0:T(1024)} %reshape.501), channel_id=1, source_target_pairs={{4,0},{8,4},{12,8},{16,12},{20,16},{24,20},{28,24},{32,28},{36,32}... | collective-permute-start | bytes 147464 | tf_op jit(solution)/shard_map/ppermute | solution.py:46
  143.9 4.1 %collective-permute-start.18 = (f32[4608]{0:T(1024)}, f32[4608]{0:T(1024)}, u32[]{:S(2)}, u32[]{:S(2)}) collective-permute-start(f32[4608]{0:T(1024)} %reshape.504), channel_id=1, source_target_pairs={{0,1},{1,2},{2,3},{4,5},{5,6},{6,7},{8,9},{9,10},{10,11},{12,13},{... | collective-permute-start | bytes 55304 | tf_op jit(solution)/shard_map/ppermute | solution.py:46
  150.0 3.8 %broadcast_multiply_fusion.1 = (f32[24,24,80]{2,1,0:T(8,128)}, f32[24,24,80]{2,1,0:T(8,128)}, f32[24,24,80]{2,1,0:T(8,128)S(1)}, f32[24,24,80]{2,1,0:T(8,128)S(1...) fusion(f32[24,24,80]{2,1,0:T(8,128)} %pad_maximum_fusion.9), kind=kLoop, calls=%fused_computation.472 | loop fusion | flops 1797120 | bytes 1658880 | tf_op jit(solution)/shard_map/mul | solution.py:119
  161.6 3.6 collective-permute-start.20
  170.5 14.3 %collective-permute-start.22 = (f32[512]{0:T(512)S(1)}, f32[512]{0:T(512)S(1)}, u32[]{:S(2)}, u32[]{:S(2)}) collective-permute-start(f32[512]{0:T(512)S(1)} %reshape.510), channel_id=1, source_target_pairs={{64,0},{128,64},{192,128},{256,192},{320,256},{384,320},{448,384},... | collective-permute-start | bytes 6152 | tf_op jit(solution)/shard_map/ppermute | solution.py:46
  187.1 3.2 collective-permute-done.23
  190.5 5.3 %collective-permute-start.24 = (f32[2560]{0:T(1024)S(1)}, f32[2560]{0:T(1024)S(1)}, u32[]{:S(2)}, u32[]{:S(2)}) collective-permute-start(f32[2560]{0:T(1024)S(1)} %reshape.515), channel_id=1, source_target_pairs={{0,8},{4,12},{8,16},{12,20},{16,24},{20,28},{24,32},{28,36},{32,40... | collective-permute-start | bytes 30728 | tf_op jit(solution)/shard_map/ppermute | solution.py:46
  195.7 2.6 collective-permute-start.25
  198.4 8.0 %collective-permute-start.26 = (f32[2560]{0:T(1024)S(1)}, f32[2560]{0:T(1024)}, u32[]{:S(2)}, u32[]{:S(2)}) collective-permute-start(f32[2560]{0:T(1024)S(1)} %reshape.515), channel_id=1, source_target_pairs={{4,0},{8,4},{12,8},{16,12},{20,16},{24,20},{28,24},{32,28},{36,32}... | collective-permute-start | bytes 30728 | tf_op jit(solution)/shard_map/ppermute | solution.py:46
  206.4 9.3 %collective-permute-start.27 = (f32[2560]{0:T(1024)S(1)}, f32[2560]{0:T(1024)S(1)}, u32[]{:S(2)}, u32[]{:S(2)}) collective-permute-start(f32[2560]{0:T(1024)S(1)} %reshape.515), channel_id=1, source_target_pairs={{8,0},{12,4},{16,8},{20,12},{24,16},{28,20},{32,24},{36,28},{40,32... | collective-permute-start | bytes 30728 | tf_op jit(solution)/shard_map/ppermute | solution.py:46
  215.7 2.1 pad_maximum_fusion.12
  218.8 1.9 collective-permute-done.27
  221.4 2.8 concatenate.110
  224.2 1.9 fusion.264
  227.2 4.5 %collective-permute-start.28 = (f32[3200]{0:T(1024)S(1)}, f32[3200]{0:T(1024)S(1)}, u32[]{:S(2)}, u32[]{:S(2)}) collective-permute-start(f32[3200]{0:T(1024)S(1)} %reshape.520), channel_id=1, source_target_pairs={{0,1},{1,2},{2,3},{4,5},{5,6},{6,7},{8,9},{9,10},{10,11},{12,13},{... | collective-permute-start | bytes 38408 | tf_op jit(solution)/shard_map/ppermute | solution.py:46
  234.2 3.8 broadcast_multiply_fusion.2
  241.3 2.0 and_select_fusion.16
  244.9 12.7 %all_gather.9 = f32[2,2,2,64]{2,1,0,3:T(2,128)S(1)} all-gather(f32[2,2,2,16]{2,1,0,3:T(2,128)S(1)} %copy.38), channel_id=1, replica_groups=mesh['gx'=8,'gy'=16,'gz'=4] {'gz'}, dimensions={3}, use_global_device_ids=true | all-gather | bytes 2560 | tf_op jit(solution)/shard_map/all_gather | solution.py:162
  257.7 12.2 %all_gather.10 = f32[2,16,2,64]{3,2,0,1:T(2,128)S(1)} all-gather(f32[2,2,2,64]{3,2,0,1:T(2,128)S(1)} %copy.39), channel_id=1, replica_groups=mesh['gx'=8,'gy'=16,'gz'=4] {'gx'}, dimensions={1}, use_global_device_ids=true | all-gather | bytes 18432 | tf_op jit(solution)/shard_map/all_gather | solution.py:162
  269.9 58.9 %all_gather.11 = f32[2,16,32,64]{3,1,0,2:T(8,128)S(1)} all-gather(f32[2,16,2,64]{3,1,0,2:T(8,128)S(1)} %copy.40), channel_id=1, replica_groups=mesh['gx'=8,'gy'=16,'gz'=4] {'gy'}, dimensions={2}, use_global_device_ids=true | all-gather | bytes 278528 | tf_op jit(solution)/shard_map/all_gather | solution.py:162
  338.2 2.1 copy.54
  346.3 1.9 copy.47
  348.2 2.1 broadcast_in_dim.85
  350.3 2.2 copy.48
  361.3 3.2 broadcast_in_dim.88
  364.5 3.6 reshape.532
  368.2 3.6 copy.50
  374.1 3.2 and_select_fusion.1
  377.3 2.0 fusion.19
  380.5 2.2 fusion.234
  (386 shorter events, 109.3 us)
Async XLA Ops:
  0.0 32.6 %copy-start.42 = (f32[16,16,128]{2,1,0:T(8,128)S(1)}, f32[16,16,128]{2,1,0:T(8,128)}, u32[]{:S(2)}) copy-start(f32[16,16,128]{2,1,0:T(8,128)} %param.3) | copy-start | bytes 393220
  5.9 26.8 %copy-start.53 = (f32[4,4,32]{2,1,0:T(4,128)}, f32[4,4,32]{2,1,0:T(4,128)S(1)}, u32[]{:S(2)}) copy-start(f32[4,4,32]{2,1,0:T(4,128)S(1)} %add_multiply_fusion.3) | copy-start | bytes 6148
  6.0 25.9 %collective-permute-start.3 = (f32[512]{0:T(512)S(1)}, f32[512]{0:T(512)S(1)}, u32[]{:S(2)}, u32[]{:S(2)}) collective-permute-start(f32[512]{0:T(512)S(1)} %reshape.458), channel_id=1, source_target_pairs={{0,128},{64,192},{128,256},{192,320},{256,384},{320,448},{1,129},{... | collective-permute-start | bytes 6152 | tf_op jit(solution)/shard_map/ppermute | solution.py:46
  9.8 22.2 %collective-permute-start.4 = (f32[512]{0:T(512)S(1)}, f32[512]{0:T(512)S(1)}, u32[]{:S(2)}, u32[]{:S(2)}) collective-permute-start(f32[512]{0:T(512)S(1)} %reshape.458), channel_id=1, source_target_pairs={{128,0},{192,64},{256,128},{320,192},{384,256},{448,320},{129,1},{... | collective-permute-start | bytes 6152 | tf_op jit(solution)/shard_map/ppermute | solution.py:46
  15.6 16.5 %collective-permute-start = (f32[29184]{0:T(1024)S(1)}, f32[29184]{0:T(1024)S(1)}, u32[]{:S(2)}, u32[]{:S(2)}) collective-permute-start(f32[29184]{0:T(1024)S(1)} %get-tuple-element.100), channel_id=1, source_target_pairs={{0,64},{64,128},{128,192},{192,256},{256,320},{320,384},{384,448},... | collective-permute-start | bytes 350216 | tf_op jit(solution)/shard_map/ppermute | solution.py:46
  17.5 14.7 %collective-permute-start.1 = (f32[29184]{0:T(1024)S(1)}, f32[29184]{0:T(1024)S(1)}, u32[]{:S(2)}, u32[]{:S(2)}) collective-permute-start(f32[29184]{0:T(1024)S(1)} %get-tuple-element.99), channel_id=1, source_target_pairs={{64,0},{128,64},{192,128},{256,192},{320,256},{384,320},{448,384},... | collective-permute-start | bytes 350216 | tf_op jit(solution)/shard_map/ppermute | solution.py:46
  21.3 5.7 %collective-permute-start.2 = (f32[128]{0:T(128)S(1)}, f32[128]{0:T(128)S(1)}, u32[]{:S(2)}, u32[]{:S(2)}) collective-permute-start(f32[128]{0:T(128)S(1)} %reshape.466), channel_id=1, source_target_pairs={{0,192},{64,256},{128,320},{192,384},{256,448},{1,193},{65,257},{1... | collective-permute-start | bytes 1544 | tf_op jit(solution)/shard_map/ppermute | solution.py:46
  25.0 7.8 %copy-start.57 = (pred[80]{0:T(512)(128)(4,1)}, pred[80]{0:T(512)(128)(4,1)S(1)}, u32[]{:S(2)}) copy-start(pred[80]{0:T(512)(128)(4,1)S(1)} %compare_and_fusion.3) | copy-start | bytes 244
  27.0 4.8 %collective-permute-start.5 = (f32[128]{0:T(128)S(1)}, f32[128]{0:T(128)S(1)}, u32[]{:S(2)}, u32[]{:S(2)}) collective-permute-start(f32[128]{0:T(128)S(1)} %reshape.472), channel_id=1, source_target_pairs={{192,0},{256,64},{320,128},{384,192},{448,256},{193,1},{257,65},{3... | collective-permute-start | bytes 1544 | tf_op jit(solution)/shard_map/ppermute | solution.py:46
  32.5 51.1 %copy-start.43 = (f32[24576]{0:T(1024)}, f32[24576]{0:T(1024)S(1)}, u32[]{:S(2)}) copy-start(f32[24576]{0:T(1024)S(1)} %slice.1092) | copy-start | bytes 294916
  32.6 51.1 %copy-start.45 = (f32[24576]{0:T(1024)}, f32[24576]{0:T(1024)S(1)}, u32[]{:S(2)}) copy-start(f32[24576]{0:T(1024)S(1)} %slice.1093) | copy-start | bytes 294916
  32.9 47.8 %copy-start.52 = (f32[8,8,64]{2,1,0:T(8,128)}, f32[8,8,64]{2,1,0:T(8,128)S(1)}, u32[]{:S(2)}) copy-start(f32[8,8,64]{2,1,0:T(8,128)S(1)} %reshape.464) | copy-start | bytes 49156
  33.0 45.2 %collective-permute-start.6 = (f32[58112]{0:T(1024)S(1)}, f32[58112]{0:T(1024)S(1)}, u32[]{:S(2)}, u32[]{:S(2)}) collective-permute-start(f32[58112]{0:T(1024)S(1)} %get-tuple-element.97), channel_id=1, source_target_pairs={{0,4},{4,8},{8,12},{12,16},{16,20},{20,24},{24,28},{28,32},{32,36}... | collective-permute-start | bytes 697352 | tf_op jit(solution)/shard_map/ppermute | solution.py:46
  42.1 36.2 %collective-permute-start.7 = (f32[58112]{0:T(1024)S(1)}, f32[58112]{0:T(1024)S(1)}, u32[]{:S(2)}, u32[]{:S(2)}) collective-permute-start(f32[58112]{0:T(1024)S(1)} %get-tuple-element.98), channel_id=1, source_target_pairs={{4,0},{8,4},{12,8},{16,12},{20,16},{24,20},{28,24},{32,28},{36,32}... | collective-permute-start | bytes 697352 | tf_op jit(solution)/shard_map/ppermute | solution.py:46
  45.3 23.2 %collective-permute-start.8 = (f32[704]{0:T(1024)S(1)}, f32[704]{0:T(1024)S(1)}, u32[]{:S(2)}, u32[]{:S(2)}) collective-permute-start(f32[704]{0:T(1024)S(1)} %reshape.482), channel_id=1, source_target_pairs={{0,12},{4,16},{8,20},{12,24},{16,28},{20,32},{24,36},{28,40},{32,4... | collective-permute-start | bytes 8456 | tf_op jit(solution)/shard_map/ppermute | solution.py:46
  53.0 25.0 %collective-permute-start.9 = (f32[2816]{0:T(1024)S(1)}, f32[2816]{0:T(1024)S(1)}, u32[]{:S(2)}, u32[]{:S(2)}) collective-permute-start(f32[2816]{0:T(1024)S(1)} %reshape.474), channel_id=1, source_target_pairs={{0,8},{4,12},{8,16},{12,20},{16,24},{20,28},{24,32},{28,36},{32,40... | collective-permute-start | bytes 33800 | tf_op jit(solution)/shard_map/ppermute | solution.py:46
  57.2 20.9 %collective-permute-start.10 = (f32[2816]{0:T(1024)S(1)}, f32[2816]{0:T(1024)S(1)}, u32[]{:S(2)}, u32[]{:S(2)}) collective-permute-start(f32[2816]{0:T(1024)S(1)} %reshape.474), channel_id=1, source_target_pairs={{8,0},{12,4},{16,8},{20,12},{24,16},{28,20},{32,24},{36,28},{40,32... | collective-permute-start | bytes 33800 | tf_op jit(solution)/shard_map/ppermute | solution.py:46
  68.5 9.4 %collective-permute-start.11 = (f32[704]{0:T(1024)S(1)}, f32[704]{0:T(1024)S(1)}, u32[]{:S(2)}, u32[]{:S(2)}) collective-permute-start(f32[704]{0:T(1024)S(1)} %reshape.488), channel_id=1, source_target_pairs={{12,0},{16,4},{20,8},{24,12},{28,16},{32,20},{36,24},{40,28},{44,3... | collective-permute-start | bytes 8456 | tf_op jit(solution)/shard_map/ppermute | solution.py:46
  84.1 9.3 %copy-start.59 = (pred[50]{0:T(512)(128)(4,1)S(1)}, pred[50]{0:T(512)(128)(4,1)}, u32[]{:S(2)}) copy-start(pred[50]{0:T(512)(128)(4,1)} %compare_and_fusion) | copy-start | bytes 154
  85.4 8.8 %collective-permute-start.12 = (f32[18372]{0:T(1024)S(1)}, f32[18372]{0:T(1024)S(1)}, u32[]{:S(2)}, u32[]{:S(2)}) collective-permute-start(f32[18372]{0:T(1024)S(1)} %concatenate.101), channel_id=1, source_target_pairs={{0,1},{1,2},{2,3},{4,5},{5,6},{6,7},{8,9},{9,10},{10,11},{12,13},{... | collective-permute-start | bytes 220472 | tf_op jit(solution)/shard_map/ppermute | solution.py:46
  90.0 8.3 %copy-start.44 = (f32[24576]{0:T(1024)S(1)}, f32[24576]{0:T(1024)}, u32[]{:S(2)}) copy-start(f32[24576]{0:T(1024)} %copy-done.43) | copy-start | bytes 294916
  90.1 8.3 %copy-start.46 = (f32[24576]{0:T(1024)S(1)}, f32[24576]{0:T(1024)}, u32[]{:S(2)}) copy-start(f32[24576]{0:T(1024)} %copy-done.45) | copy-start | bytes 294916
  91.8 6.2 %collective-permute-start.13 = (f32[18372]{0:T(1024)S(1)}, f32[18372]{0:T(1024)S(1)}, u32[]{:S(2)}, u32[]{:S(2)}) collective-permute-start(f32[18372]{0:T(1024)S(1)} %concatenate.102), channel_id=1, source_target_pairs={{1,0},{2,1},{3,2},{5,4},{6,5},{7,6},{9,8},{10,9},{11,10},{13,12},{... | collective-permute-start | bytes 220472 | tf_op jit(solution)/shard_map/ppermute | solution.py:46
  94.2 5.2 %copy-start.55 = (f32[18372]{0:T(1024)}, f32[18372]{0:T(1024)S(1)}, u32[]{:S(2)}) copy-start(f32[18372]{0:T(1024)S(1)} %collective-permute-done.12) | copy-start | bytes 220468
  99.6 7.8 %copy-start.47 = (f32[28,28,140]{2,1,0:T(8,128)}, f32[28,28,140]{2,1,0:T(8,128)S(1)}, u32[]{:S(2)}) copy-start(f32[28,28,140]{2,1,0:T(8,128)S(1)} %get-tuple-element.58) | copy-start | bytes 1317124
  102.2 5.2 %copy-start.4 = (f32[28,28,140]{2,1,0:T(8,128)}, f32[28,28,140]{2,1,0:T(8,128)S(1)}, u32[]{:S(2)}) copy-start(f32[28,28,140]{2,1,0:T(8,128)S(1)} %get-tuple-element.15) | copy-start | bytes 1317124
  102.2 5.2 %copy-start.6 = (f32[28,28,140]{2,1,0:T(8,128)}, f32[28,28,140]{2,1,0:T(8,128)S(1)}, u32[]{:S(2)}) copy-start(f32[28,28,140]{2,1,0:T(8,128)S(1)} %get-tuple-element.16) | copy-start | bytes 1317124
  102.2 5.2 %copy-start.8 = (f32[28,28,140]{2,1,0:T(8,128)}, f32[28,28,140]{2,1,0:T(8,128)S(1)}, u32[]{:S(2)}) copy-start(f32[28,28,140]{2,1,0:T(8,128)S(1)} %get-tuple-element.10) | copy-start | bytes 1317124
  107.3 8.1 %copy-start.54 = (f32[4,4,32]{2,1,0:T(4,128)S(1)}, f32[4,4,32]{2,1,0:T(4,128)}, u32[]{:S(2)}) copy-start(f32[4,4,32]{2,1,0:T(4,128)} %copy-done.53) | copy-start | bytes 6148
  107.4 29.3 %copy-start.49 = (f32[24,8,64]{2,1,0:T(8,128)S(1)}, f32[24,8,64]{2,1,0:T(8,128)}, u32[]{:S(2)}) copy-start(f32[24,8,64]{2,1,0:T(8,128)} %copy-done.48) | copy-start | bytes 147460
  109.2 30.2 %copy-start.51 = (f32[8,8,64]{2,1,0:T(8,128)}, f32[8,8,64]{2,1,0:T(8,128)S(1)}, u32[]{:S(2)}) copy-start(f32[8,8,64]{2,1,0:T(8,128)S(1)} %add_multiply_fusion) | copy-start | bytes 49156
  109.9 10.3 %collective-permute-start.14 = (f32[4096]{0:T(1024)}, f32[4096]{0:T(1024)}, u32[]{:S(2)}, u32[]{:S(2)}) collective-permute-start(f32[4096]{0:T(1024)} %reshape.498), channel_id=1, source_target_pairs={{0,64},{64,128},{128,192},{192,256},{256,320},{320,384},{384,448},... | collective-permute-start | bytes 49160 | tf_op jit(solution)/shard_map/ppermute | solution.py:46
  111.8 9.8 %collective-permute-start.15 = (f32[4096]{0:T(1024)}, f32[4096]{0:T(1024)}, u32[]{:S(2)}, u32[]{:S(2)}) collective-permute-start(f32[4096]{0:T(1024)} %reshape.498), channel_id=1, source_target_pairs={{64,0},{128,64},{192,128},{256,192},{320,256},{384,320},{448,384},... | collective-permute-start | bytes 49160 | tf_op jit(solution)/shard_map/ppermute | solution.py:46
  126.0 12.5 %collective-permute-start.16 = (f32[12288]{0:T(1024)}, f32[12288]{0:T(1024)}, u32[]{:S(2)}, u32[]{:S(2)}) collective-permute-start(f32[12288]{0:T(1024)} %reshape.501), channel_id=1, source_target_pairs={{0,4},{4,8},{8,12},{12,16},{16,20},{20,24},{24,28},{28,32},{32,36}... | collective-permute-start | bytes 147464 | tf_op jit(solution)/shard_map/ppermute | solution.py:46
  127.9 13.4 %collective-permute-start.17 = (f32[12288]{0:T(1024)}, f32[12288]{0:T(1024)}, u32[]{:S(2)}, u32[]{:S(2)}) collective-permute-start(f32[12288]{0:T(1024)} %reshape.501), channel_id=1, source_target_pairs={{4,0},{8,4},{12,8},{16,12},{20,16},{24,20},{28,24},{32,28},{36,32}... | collective-permute-start | bytes 147464 | tf_op jit(solution)/shard_map/ppermute | solution.py:46
  143.9 10.0 %collective-permute-start.18 = (f32[4608]{0:T(1024)}, f32[4608]{0:T(1024)}, u32[]{:S(2)}, u32[]{:S(2)}) collective-permute-start(f32[4608]{0:T(1024)} %reshape.504), channel_id=1, source_target_pairs={{0,1},{1,2},{2,3},{4,5},{5,6},{6,7},{8,9},{9,10},{10,11},{12,13},{... | collective-permute-start | bytes 55304 | tf_op jit(solution)/shard_map/ppermute | solution.py:46
  148.7 6.8 %collective-permute-start.19 = (f32[4608]{0:T(1024)}, f32[4608]{0:T(1024)}, u32[]{:S(2)}, u32[]{:S(2)}) collective-permute-start(f32[4608]{0:T(1024)} %reshape.506), channel_id=1, source_target_pairs={{1,0},{2,1},{3,2},{5,4},{6,5},{7,6},{9,8},{10,9},{11,10},{13,12},{... | collective-permute-start | bytes 55304 | tf_op jit(solution)/shard_map/ppermute | solution.py:46
  161.6 25.2 %collective-permute-start.20 = (f32[512]{0:T(512)S(1)}, f32[512]{0:T(512)S(1)}, u32[]{:S(2)}, u32[]{:S(2)}) collective-permute-start(f32[512]{0:T(512)S(1)} %reshape.510), channel_id=1, source_target_pairs={{0,128},{64,192},{128,256},{192,320},{256,384},{320,448},{1,129},{... | collective-permute-start | bytes 6152 | tf_op jit(solution)/shard_map/ppermute | solution.py:46
  168.6 18.3 %collective-permute-start.21 = (f32[512]{0:T(512)S(1)}, f32[512]{0:T(512)S(1)}, u32[]{:S(2)}, u32[]{:S(2)}) collective-permute-start(f32[512]{0:T(512)S(1)} %reshape.510), channel_id=1, source_target_pairs={{0,64},{64,128},{128,192},{192,256},{256,320},{320,384},{384,448},... | collective-permute-start | bytes 6152 | tf_op jit(solution)/shard_map/ppermute | solution.py:46
  170.5 16.5 %collective-permute-start.22 = (f32[512]{0:T(512)S(1)}, f32[512]{0:T(512)S(1)}, u32[]{:S(2)}, u32[]{:S(2)}) collective-permute-start(f32[512]{0:T(512)S(1)} %reshape.510), channel_id=1, source_target_pairs={{64,0},{128,64},{192,128},{256,192},{320,256},{384,320},{448,384},... | collective-permute-start | bytes 6152 | tf_op jit(solution)/shard_map/ppermute | solution.py:46
  184.8 5.5 %collective-permute-start.23 = (f32[512]{0:T(512)S(1)}, f32[512]{0:T(512)S(1)}, u32[]{:S(2)}, u32[]{:S(2)}) collective-permute-start(f32[512]{0:T(512)S(1)} %reshape.510), channel_id=1, source_target_pairs={{128,0},{192,64},{256,128},{320,192},{384,256},{448,320},{129,1},{... | collective-permute-start | bytes 6152 | tf_op jit(solution)/shard_map/ppermute | solution.py:46
  190.5 27.3 %collective-permute-start.24 = (f32[2560]{0:T(1024)S(1)}, f32[2560]{0:T(1024)S(1)}, u32[]{:S(2)}, u32[]{:S(2)}) collective-permute-start(f32[2560]{0:T(1024)S(1)} %reshape.515), channel_id=1, source_target_pairs={{0,8},{4,12},{8,16},{12,20},{16,24},{20,28},{24,32},{28,36},{32,40... | collective-permute-start | bytes 30728 | tf_op jit(solution)/shard_map/ppermute | solution.py:46
  195.7 22.1 %collective-permute-start.25 = (f32[2560]{0:T(1024)S(1)}, f32[2560]{0:T(1024)S(1)}, u32[]{:S(2)}, u32[]{:S(2)}) collective-permute-start(f32[2560]{0:T(1024)S(1)} %reshape.515), channel_id=1, source_target_pairs={{0,4},{4,8},{8,12},{12,16},{16,20},{20,24},{24,28},{28,32},{32,36}... | collective-permute-start | bytes 30728 | tf_op jit(solution)/shard_map/ppermute | solution.py:46
  198.4 19.6 %collective-permute-start.26 = (f32[2560]{0:T(1024)S(1)}, f32[2560]{0:T(1024)}, u32[]{:S(2)}, u32[]{:S(2)}) collective-permute-start(f32[2560]{0:T(1024)S(1)} %reshape.515), channel_id=1, source_target_pairs={{4,0},{8,4},{12,8},{16,12},{20,16},{24,20},{28,24},{32,28},{36,32}... | collective-permute-start | bytes 30728 | tf_op jit(solution)/shard_map/ppermute | solution.py:46
  206.4 14.3 %collective-permute-start.27 = (f32[2560]{0:T(1024)S(1)}, f32[2560]{0:T(1024)S(1)}, u32[]{:S(2)}, u32[]{:S(2)}) collective-permute-start(f32[2560]{0:T(1024)S(1)} %reshape.515), channel_id=1, source_target_pairs={{8,0},{12,4},{16,8},{20,12},{24,16},{28,20},{32,24},{36,28},{40,32... | collective-permute-start | bytes 30728 | tf_op jit(solution)/shard_map/ppermute | solution.py:46
  226.1 13.5 %copy-start.60 = (pred[50]{0:T(512)(128)(4,1)S(1)}, pred[50]{0:T(512)(128)(4,1)}, u32[]{:S(2)}) copy-start(pred[50]{0:T(512)(128)(4,1)} %compare_and_fusion) | copy-start | bytes 154
  227.2 10.8 %collective-permute-start.28 = (f32[3200]{0:T(1024)S(1)}, f32[3200]{0:T(1024)S(1)}, u32[]{:S(2)}, u32[]{:S(2)}) collective-permute-start(f32[3200]{0:T(1024)S(1)} %reshape.520), channel_id=1, source_target_pairs={{0,1},{1,2},{2,3},{4,5},{5,6},{6,7},{8,9},{9,10},{10,11},{12,13},{... | collective-permute-start | bytes 38408 | tf_op jit(solution)/shard_map/ppermute | solution.py:46
  232.9 6.0 %collective-permute-start.29 = (f32[3200]{0:T(1024)S(1)}, f32[3200]{0:T(1024)S(1)}, u32[]{:S(2)}, u32[]{:S(2)}) collective-permute-start(f32[3200]{0:T(1024)S(1)} %reshape.522), channel_id=1, source_target_pairs={{1,0},{2,1},{3,2},{5,4},{6,5},{7,6},{9,8},{10,9},{11,10},{13,12},{... | collective-permute-start | bytes 38408 | tf_op jit(solution)/shard_map/ppermute | solution.py:46
  (45 other events, 110.2 us)
